TPU v7x, 32 devices: a whole 2x2x4 slice. The times are simulated.
32 devices in a mesh: grp: 2 (over x), lat: 16 (over z, y, core).
Axes of the slice: x: 2, y: 2, z: 4, core: 2. Of those that a mesh axis runs over, the one named last changes fastest.
Arguments:
- activations: bfloat16 [64, 1440, 384], P(('grp', 'lat')), parts along dimension 0, may hold values from -6 to 6
- upstream: bfloat16 [64, 1440, 384], P(('grp', 'lat')), parts along dimension 0, may hold values from -6 to 6
- skip_weight: bfloat16 [384, 384], replicated, may hold values from -0.3125 to 0.3125
- spectral_weight: bfloat16 [32, 2, 384, 384], P('lat'), may hold values from -2.5 to 2.5
- slot_degree: int32 [32], replicated, may hold values from 0 to 31, each once
Outputs:
- grad_activations: bfloat16 [64, 1440, 384], P(('grp', 'lat')), parts along dimension 0
- grad_spectral: bfloat16 [64, 2, 384, 384], P(('grp', 'lat')), parts along dimension 0
- grad_skip: float32 [768, 384], P(('grp', 'lat')), parts along dimension 0
There are 2 independent parts, one for each index of `grp`. A program takes and returns all parts, laid end to end along the dimension named above; an argument that names none is the same for every part. Nothing has to cross between parts.
Inputs may be any that keep to these rules, and one draw needn't show every extreme that they name: `slot_degree`: device d holds slots d * 2 to (d + 1) * 2 - 1 of spectral_weight and grad_spectral; every degree appears in exactly one slot.
All inputs are finite; a program needn't handle non-finite values.
Results may differ from a plain program's by a relative error of at most 0.013.
Values may be sent and summed in bfloat16 or wider, within the bound.
No kernel may reach another device: no remote copies, remote signals or barrier semaphores. Data moves between devices by JAX's collectives and lax.ppermute only.
A program may use at most 64 MiB of HBM per device.

v0:
```python
import math
import jax
import jax.numpy as jnp
from jax import lax
from jax.sharding import PartitionSpec as P

ORDERS = 4
highest = lax.Precision.HIGHEST


def fourier_table(lon_total, orders):
    lon_ids = jnp.arange(lon_total, dtype=jnp.int32)[:, None]
    order_ids = jnp.arange(orders, dtype=jnp.int32)[None, :]
    angles = (lon_ids * order_ids % lon_total).astype(jnp.float32) * (2.0 * math.pi / lon_total)
    amplitude = math.sqrt(2.0 / lon_total)
    return jnp.concatenate(
        [amplitude * jnp.cos(angles), -amplitude * jnp.sin(angles)], axis=1
    ).astype(jnp.bfloat16)


def colatitudes(row_ids, lat_total):
    mirror = jnp.minimum(row_ids, lat_total - 1 - row_ids)
    colatitude = (mirror.astype(jnp.float32) + 0.5) * (math.pi / lat_total)
    cosines = jnp.where(row_ids < lat_total // 2, jnp.cos(colatitude), -jnp.cos(colatitude))
    return (cosines, jnp.sin(colatitude))


def legendre_table(cosines, sines, degrees, orders):
    order_col = jnp.arange(orders, dtype=jnp.float32)[:, None]
    factors = [math.sqrt(0.5)]
    for order_num in range(1, orders):
        factors.append(factors[-1] * math.sqrt((2.0 * order_num + 1.0) / (2.0 * order_num)))
    diagonal_start = jnp.array(factors, dtype=jnp.float32)[:, None] * jnp.power(
        sines[None, :], order_col
    )
    next_start = jnp.sqrt(2.0 * order_col + 3.0) * cosines[None, :] * diagonal_start

    def advance(state_pair, degree):
        previous, earlier = state_pair
        deg_value = degree.astype(jnp.float32)
        deg_below = deg_value - 1.0
        ratio_up = jnp.sqrt(
            jnp.maximum(4.0 * deg_value * deg_value - 1.0, 1.0)
            / jnp.maximum(deg_value * deg_value - order_col * order_col, 1.0)
        )
        ratio_down = jnp.sqrt(
            jnp.maximum(deg_below * deg_below - order_col * order_col, 0.0)
            / jnp.maximum(4.0 * deg_below * deg_below - 1.0, 1.0)
        )
        recurred = ratio_up * (cosines[None, :] * previous - ratio_down * earlier)
        current = jnp.where(
            deg_value == order_col,
            diagonal_start,
            jnp.where(
                deg_value == order_col + 1.0,
                next_start,
                jnp.where(deg_value > order_col + 1.0, recurred, 0.0),
            ),
        )
        return ((current, previous), current)

    zeroed = jnp.zeros((orders, cosines.shape[0]), jnp.float32)
    _, stacked = lax.scan(advance, (zeroed, zeroed), jnp.arange(degrees, dtype=jnp.int32))
    return jnp.concatenate([stacked, stacked], axis=1)


def gelu_tanh(values):
    return jax.nn.gelu(values, approximate=True)


def complex_apply(coeffs, weights, orders):
    real_in, imag_in = (coeffs[:, :orders], coeffs[:, orders:])
    real_w, imag_w = (weights[:, 0], weights[:, 1])

    def complex_term(operand_a, operand_b):
        return jnp.einsum("smc,scd->smd", operand_a, operand_b, preferred_element_type=jnp.float32)

    real_out = complex_term(real_in, real_w) - complex_term(imag_in, imag_w)
    imag_out = complex_term(real_in, imag_w) + complex_term(imag_in, real_w)
    return jnp.concatenate([real_out, imag_out], axis=1)


def complex_adjoint(coeffs, cotangents, weights, orders):
    real_in, imag_in = (coeffs[:, :orders], coeffs[:, orders:])
    real_g, imag_g = (cotangents[:, :orders], cotangents[:, orders:])
    real_w, imag_w = (weights[:, 0], weights[:, 1])

    def outer_sum(operand_a, operand_b):
        return jnp.einsum("smc,smd->scd", operand_a, operand_b, preferred_element_type=jnp.float32)

    def back_term(operand_a, operand_b):
        return jnp.einsum("smd,scd->smc", operand_a, operand_b, preferred_element_type=jnp.float32)

    grad_real = outer_sum(real_in, real_g) + outer_sum(imag_in, imag_g)
    grad_imag = outer_sum(real_in, imag_g) - outer_sum(imag_in, real_g)
    back_real = back_term(real_g, real_w) + back_term(imag_g, imag_w)
    back_imag = back_term(imag_g, real_w) - back_term(real_g, imag_w)
    return (
        jnp.stack([grad_real, grad_imag], axis=1),
        jnp.concatenate([back_real, back_imag], axis=1),
    )


def local(activations, upstream, skip_weight, spectral_weight, slot_degree):
    groups = lax.axis_size("lat")
    lat_rows = activations.shape[0]
    lon_total = activations.shape[1]
    lat_total = lat_rows * groups
    per_owner = spectral_weight.shape[0]
    degrees = per_owner * groups
    orders = ORDERS
    fourier = fourier_table(lon_total, orders)
    spectrum = jnp.einsum("jkc,kf->jfc", activations, fourier, preferred_element_type=jnp.float32)
    all_rows = jnp.arange(lat_total, dtype=jnp.int32)
    cos_all, sin_all = colatitudes(all_rows, lat_total)
    slot_plm = jnp.take(legendre_table(cos_all, sin_all, degrees, orders), slot_degree, axis=0)
    slot_quad = slot_plm * (math.pi / lat_total * sin_all)[None, None, :]

    def to_channels(values):
        return lax.all_to_all(values, "lat", split_axis=2, concat_axis=0, tiled=True)

    def to_owners(values):
        return lax.all_to_all(values, "lat", split_axis=0, concat_axis=2, tiled=True)

    def from_owners(values):
        return lax.all_to_all(values, "lat", split_axis=2, concat_axis=0, tiled=True)

    def to_rows(values):
        return lax.all_to_all(values, "lat", split_axis=0, concat_axis=2, tiled=True)

    by_channel = to_channels(spectrum)
    coeffs = to_owners(
        jnp.einsum("sfj,jfc->sfc", slot_quad, by_channel, precision=highest).astype(jnp.bfloat16)
    )
    filtered = complex_apply(coeffs, spectral_weight, orders).astype(jnp.bfloat16)
    spread = from_owners(filtered).astype(jnp.float32)
    grid_modes = to_rows(
        jnp.einsum("sfj,sfc->jfc", slot_plm, spread, precision=highest).astype(jnp.bfloat16)
    )
    spatial = jnp.einsum("jfc,kf->jkc", grid_modes, fourier, preferred_element_type=jnp.float32)
    skip_out = jnp.einsum(
        "jkc,cd->jkd", activations, skip_weight, preferred_element_type=jnp.float32
    )
    _, pullback = jax.vjp(gelu_tanh, spatial + skip_out)
    slope_b = pullback(upstream.astype(jnp.float32))[0].astype(jnp.bfloat16)
    grad_skip = lax.psum_scatter(
        jnp.einsum("jkc,jkd->cd", activations, slope_b, preferred_element_type=jnp.float32),
        "lat",
        scatter_dimension=0,
        tiled=True,
    ) * (1.0 / math.sqrt(lat_total * lon_total))
    through_skip = jnp.einsum(
        "jkd,cd->jkc", slope_b, skip_weight, preferred_element_type=jnp.float32
    )
    mode_grads = jnp.einsum("jkc,kf->jfc", slope_b, fourier, preferred_element_type=jnp.float32)
    grads_by_channel = to_channels(mode_grads)
    coeff_grads = to_owners(
        jnp.einsum("sfj,jfc->sfc", slot_plm, grads_by_channel, precision=highest).astype(
            jnp.bfloat16
        )
    )
    weight_grads, back_coeffs = complex_adjoint(coeffs, coeff_grads, spectral_weight, orders)
    back_b = back_coeffs.astype(jnp.bfloat16)
    back_spread = from_owners(back_b).astype(jnp.float32)
    row_grads = to_rows(
        jnp.einsum("sfj,sfc->jfc", slot_quad, back_spread, precision=highest).astype(jnp.bfloat16)
    )
    through_modes = jnp.einsum(
        "jfc,kf->jkc", row_grads, fourier, preferred_element_type=jnp.float32
    )
    grad_activations = (upstream.astype(jnp.float32) + through_skip + through_modes).astype(
        jnp.bfloat16
    )
    return (grad_activations, weight_grads.astype(jnp.bfloat16), grad_skip)


def solution(mesh):
    in_specs = (
        P(("grp", "lat"), None, None),
        P(("grp", "lat"), None, None),
        P(),
        P("lat", None, None, None),
        P(),
    )
    out_specs = (
        P(("grp", "lat"), None, None),
        P(("grp", "lat"), None, None, None),
        P(("grp", "lat"), None),
    )
    return jax.shard_map(local, mesh=mesh, in_specs=in_specs, out_specs=out_specs, check_vma=False)
```

profile of v0, /device:TPU:0, one launch (start us, length us, event | category | flops | bytes accessed | tf_op | source)
XLA Modules:
  0.0 300.9 jit_solution(992449923088837298)
XLA Ops:
  9.2 0.9 copy.49
  10.1 2.2 reshape.143
  12.3 7.4 %all-to-all-start = ((f32[16,1,384]{2,1,0:T(1,128)}), f32[16,1,384]{2,1,0:T(1,128)}, u32[]{:S(2)}, u32[]{:S(2)}) async-start(f32[16,1,384]{2,1,0:T(1,128)} %reshape.143), calls=%async_computation | async-start | bytes 49152 | tf_op jit(solution)/shard_map/all_to_all | solution.py:120
  20.0 67.6 %while.21 = (s32[]{:T(128)}, f32[4,32]{1,0:T(4,128)S(1)}, f32[4,32]{1,0:T(4,128)S(1)}, f32[32,4,32]{2,1,0:T(4,128)}, s32[32]{0:T(128)S(1)}, /*index=5*/f32[32]{0...) while((s32[]{:T(128)}, f32[4,32]{1,0:T(4,128)S(1)}, ...), condition=%wide.region_1.2_spmd.clone.clone.clone.clone, body=%wide.region_0.1_spmd.clone.clone.clone.clone.sunk | while | flops 1723 | bytes 5059 | solution.py:63
  87.6 1.0 pad_maximum_fusion.1
  88.5 1.2 gather_fusion
  89.8 1.7 broadcast_multiply_fusion
  91.9 2.0 reduce
  93.9 2.1 reshape.144
  96.0 1.8 copy.50
  97.8 1.9 fusion.43
  99.7 1.5 copy.53
  101.3 1.6 reshape.145
  102.8 12.4 %all_to_all.144 = bf16[16,2,192]{2,1,0:T(2,128)(2,1)} all-to-all(bf16[16,2,192]{2,1,0:T(2,128)(2,1)} %reshape.145), channel_id=1, replica_groups=mesh['grp'=2,'lat'=16] {'lat'}, dimensions={0} | all-to-all | bytes 24576 | tf_op jit(solution)/shard_map/all_to_all | solution.py:123
  115.2 1.5 reshape.146
  116.7 1.5 copy.54
  118.2 1.0 all_to_all.111
  120.6 1.6 copy.57
  122.1 1.8 reshape.147
  123.9 10.5 %all_to_all.145 = bf16[16,2,192]{2,1,0:T(2,128)(2,1)} all-to-all(bf16[16,2,192]{2,1,0:T(2,128)(2,1)} %reshape.147), channel_id=1, replica_groups=mesh['grp'=2,'lat'=16] {'lat'}, dimensions={0} | all-to-all | bytes 24576 | tf_op jit(solution)/shard_map/all_to_all | solution.py:126
  134.4 1.6 reshape.148
  135.9 1.7 copy.58
  137.6 1.8 fusion.44
  139.5 1.5 copy.61
  141.0 1.6 reshape.149
  142.6 10.5 %all_to_all.146 = bf16[16,2,192]{2,1,0:T(2,128)(2,1)} all-to-all(bf16[16,2,192]{2,1,0:T(2,128)(2,1)} %reshape.149), channel_id=1, replica_groups=mesh['grp'=2,'lat'=16] {'lat'}, dimensions={0} | all-to-all | bytes 24576 | tf_op jit(solution)/shard_map/all_to_all | solution.py:129
  153.0 1.5 reshape.150
  154.5 1.5 copy.62
  156.0 1.6 all_to_all.119
  157.6 1.7 fusion.109
  159.2 4.4 %fusion.33 = bf16[2,1440,384]{2,1,0:T(8,128)(2,1)S(1)} fusion(bf16[2,1440,384]{2,1,0:T(8,128)(2,1)S(1)} %copy-done.5, f32[1440,2,384]{2,0,1:T(8,128)S(1)} %fusion.109, bf16[2,1440,384]{2,1,0:T(8,128)(2,1)S(1)} %copy-done, bf16[384,384]{1,0:T(8,128)(2,1)S(1)} %copy-done.12), kind=kOutput, calls=%fused_computation.45 | convolution fusion | flops 873676800 | bytes 11354112 | tf_op jit(solution)/shard_map/jkc,cd->jkd/dot_general | solution.py:141
  163.7 1.3 copy-done.1
  165.0 1.0 convolution_bitcast_fusion.1
  166.1 1.6 copy.63
  167.7 2.2 reshape.151
  169.9 4.1 %all-to-all-start.4 = ((f32[16,1,384]{2,1,0:T(1,128)}), f32[16,1,384]{2,1,0:T(1,128)}, u32[]{:S(2)}, u32[]{:S(2)}) async-start(f32[16,1,384]{2,1,0:T(1,128)} %reshape.151), calls=%async_computation.4 | async-start | bytes 49152 | tf_op jit(solution)/shard_map/all_to_all | solution.py:120
  175.3 5.3 %all-to-all-done.4 = f32[16,1,384]{2,1,0:T(1,128)} async-done(((f32[16,1,384]{2,1,0:T(1,128)}), f32[16,1,384]{2,1,0:T(1,128)}, u32[]{:S(2)}, u32[]{:S(2)}) %all-to-all-start.4) | async-done | bytes 24608 | tf_op jit(solution)/shard_map/all_to_all | solution.py:120
  180.6 2.0 reduce.1
  182.6 2.1 reshape.152
  184.7 1.8 copy.64
  186.5 2.0 fusion.45
  188.5 1.5 copy.67
  190.0 1.6 reshape.153
  191.6 3.5 %all-to-all-start.5 = ((bf16[16,2,192]{2,1,0:T(2,128)(2,1)}), bf16[16,2,192]{2,1,0:T(2,128)(2,1)S(1)}, u32[]{:S(2)}, u32[]{:S(2)}) async-start(bf16[16,2,192]{2,1,0:T(2,128)(2,1)} %reshape.153), calls=%async_computation.5 | async-start | bytes 32768 | tf_op jit(solution)/shard_map/all_to_all | solution.py:123
  195.3 3.8 %convolution_bitcast_fusion = f32[384,384]{0,1:T(8,128)} fusion(bf16[2,1440,384]{2,1,0:T(8,128)(2,1)} %copy-done.1, bf16[2,1440,384]{2,1,0:T(8,128)(2,1)S(1)} %copy-done), kind=kOutput, calls=%fused_computation.56 | convolution fusion | flops 849346560 | bytes 5013504 | tf_op jit(solution)/shard_map/jkc,jkd->cd/dot_general | solution.py:147
  199.2 2.4 all-to-all-done.5
  202.3 1.5 copy.68
  203.7 1.0 all_to_all.127
  205.2 1.4 fusion.86
  206.7 1.4 fusion.92
  209.3 1.5 copy.69
  210.8 1.8 reshape.155
  212.6 4.1 %all-to-all-start.6 = ((bf16[16,2,192]{2,1,0:T(2,128)(2,1)}), bf16[16,2,192]{2,1,0:T(2,128)(2,1)}, u32[]{:S(2)}, u32[]{:S(2)}) async-start(bf16[16,2,192]{2,1,0:T(2,128)(2,1)} %reshape.155), calls=%async_computation.6 | async-start | bytes 32768 | tf_op jit(solution)/shard_map/all_to_all | solution.py:126
  216.6 2.5 fusion.41
  219.1 1.2 fusion.42
  220.3 2.9 all-to-all-done.6
  223.2 0.9 reshape.156
  225.4 3.5 %all-to-all-start.7 = ((bf16[16,2,192]{2,1,0:T(2,128)(2,1)}), bf16[16,2,192]{2,1,0:T(2,128)(2,1)S(1)}, u32[]{:S(2)}, u32[]{:S(2)}) async-start(bf16[16,2,192]{2,1,0:T(2,128)(2,1)} %reshape.157), calls=%async_computation.7 | async-start | bytes 32768 | tf_op jit(solution)/shard_map/all_to_all | solution.py:129
  228.9 1.4 pad_maximum_fusion
  230.3 1.1 copy.75
  231.5 3.9 %all-to-all-done.7 = bf16[16,2,192]{2,1,0:T(2,128)(2,1)S(1)} async-done(((bf16[16,2,192]{2,1,0:T(2,128)(2,1)}), bf16[16,2,192]{2,1,0:T(2,128)(2,1)S(1)}, u32[]{:S(2)}, u32[]{:S(2)}) %all-to-all-start.7) | async-done | bytes 12320 | tf_op jit(solution)/shard_map/all_to_all | solution.py:129
  238.0 3.9 %fusion.38 = bf16[2,1440,384]{2,1,0:T(8,128)(2,1)} fusion(bf16[2,1440,384]{2,1,0:T(8,128)(2,1)S(1)} %copy-done.6, f32[1440,2,384]{2,0,1:T(8,128)S(1)} %fusion.108, bf16[2,1440,384]{2,1,0:T(8,128)(2,1)S(1)} %copy-done.2, bf16[384,384]{1,0:T(8,128)(2,1)} %param.10), kind=kOutput, calls=%fused_computation.50 | convolution fusion | flops 853770240 | bytes 11354112 | tf_op jit(solution)/shard_map/jkd,cd->jkc/dot_general | solution.py:152
  241.9 50.3 %all-reduce.3.cloned.1.call-done = f32[384,384]{0,1:T(8,128)} async-done(((f32[384,384]{0,1:T(8,128)}), f32[384,384]{0,1:T(8,128)}) %all-reduce.3.cloned.1.call-update) | async-done | bytes 589840
  292.2 1.1 dynamic-slice_multiply_fusion
  (260 shorter events, 56.7 us)
Async XLA Ops:
  7.2 1.7 copy-start
  7.2 12.8 %copy-start.13 = (f32[4]{0:T(128)S(1)}, f32[4]{0:T(128)}, u32[]{:S(2)}) copy-start(f32[4]{0:T(128)} %constant.106.clone) | copy-start | bytes 52
  7.2 12.7 %copy-start.14 = (s32[32]{0:T(128)S(1)}, s32[32]{0:T(128)}, u32[]{:S(2)}) copy-start(s32[32]{0:T(128)} %param.12) | copy-start | bytes 388
  7.4 0.6 copy-start.9
  7.4 156.2 %copy-start.7 = (bf16[1440,4]{0,1:T(4,128)(2,1)}, bf16[1440,4]{0,1:T(4,128)(2,1)S(1)}, u32[]{:S(2)}) copy-start(bf16[1440,4]{0,1:T(4,128)(2,1)S(1)} %get-tuple-element.333) | copy-start | bytes 34564
  9.2 109.9 %copy-start.3 = (bf16[2,2,384,384]{3,2,1,0:T(8,128)(2,1)S(1)}, bf16[2,2,384,384]{3,2,1,0:T(8,128)(2,1)}, u32[]{:S(2)}) copy-start(bf16[2,2,384,384]{3,2,1,0:T(8,128)(2,1)} %param.11) | copy-start | bytes 3538948
  12.3 79.1 %all-to-all-start = ((f32[16,1,384]{2,1,0:T(1,128)}), f32[16,1,384]{2,1,0:T(1,128)}, u32[]{:S(2)}, u32[]{:S(2)}) async-start(f32[16,1,384]{2,1,0:T(1,128)} %reshape.143), calls=%async_computation | async-start | bytes 49152 | tf_op jit(solution)/shard_map/all_to_all | solution.py:120
  157.6 1.7 copy-start.5
  157.6 1.7 copy-start.12
  159.2 5.8 %copy-start.10 = (bf16[1440,4]{0,1:T(4,128)(2,1)S(1)}, bf16[1440,4]{0,1:T(4,128)(2,1)}, u32[]{:S(2)}) copy-start(bf16[1440,4]{0,1:T(4,128)(2,1)} %copy-done.9) | copy-start | bytes 34564
  163.7 1.4 copy-start.1
  165.0 9.0 %copy-start.15 = (u32[32]{0:T(128)S(1)}, u32[32]{0:T(128)}, u32[]{:S(2)}) copy-start(u32[32]{0:T(128)} %constant.112) | copy-start | bytes 388
  169.9 10.7 %all-to-all-start.4 = ((f32[16,1,384]{2,1,0:T(1,128)}), f32[16,1,384]{2,1,0:T(1,128)}, u32[]{:S(2)}, u32[]{:S(2)}) async-start(f32[16,1,384]{2,1,0:T(1,128)} %reshape.151), calls=%async_computation.4 | async-start | bytes 49152 | tf_op jit(solution)/shard_map/all_to_all | solution.py:120
  191.6 10.0 %all-to-all-start.5 = ((bf16[16,2,192]{2,1,0:T(2,128)(2,1)}), bf16[16,2,192]{2,1,0:T(2,128)(2,1)S(1)}, u32[]{:S(2)}, u32[]{:S(2)}) async-start(bf16[16,2,192]{2,1,0:T(2,128)(2,1)} %reshape.153), calls=%async_computation.5 | async-start | bytes 32768 | tf_op jit(solution)/shard_map/all_to_all | solution.py:123
  195.1 97.1 %all-reduce.3.cloned.1.call-start = ((), (), s32[]{:S(2)}) async-start(), calls=%async_computation.8 | async-start | bytes 1179648
  208.6 10.5 %copy-start.4 = (f32[2,384,384]{2,1,0:T(8,128)S(1)}, f32[2,384,384]{2,1,0:T(8,128)}, u32[]{:S(2)}) copy-start(f32[2,384,384]{2,1,0:T(8,128)} %fusion.92) | copy-start | bytes 3538948
  212.6 10.6 %all-to-all-start.6 = ((bf16[16,2,192]{2,1,0:T(2,128)(2,1)}), bf16[16,2,192]{2,1,0:T(2,128)(2,1)}, u32[]{:S(2)}, u32[]{:S(2)}) async-start(bf16[16,2,192]{2,1,0:T(2,128)(2,1)} %reshape.155), calls=%async_computation.6 | async-start | bytes 32768 | tf_op jit(solution)/shard_map/all_to_all | solution.py:126
  225.4 10.0 %all-to-all-start.7 = ((bf16[16,2,192]{2,1,0:T(2,128)(2,1)}), bf16[16,2,192]{2,1,0:T(2,128)(2,1)S(1)}, u32[]{:S(2)}, u32[]{:S(2)}) async-start(bf16[16,2,192]{2,1,0:T(2,128)(2,1)} %reshape.157), calls=%async_computation.7 | async-start | bytes 32768 | tf_op jit(solution)/shard_map/all_to_all | solution.py:129
  228.9 6.7 %copy-start.8 = (bf16[1440,4]{0,1:T(4,128)(2,1)S(1)}, bf16[1440,4]{0,1:T(4,128)(2,1)}, u32[]{:S(2)}) copy-start(bf16[1440,4]{0,1:T(4,128)(2,1)} %copy-done.7) | copy-start | bytes 34564
  228.9 6.7 %copy-start.11 = (bf16[1440,4]{0,1:T(4,128)(2,1)S(1)}, bf16[1440,4]{0,1:T(4,128)(2,1)}, u32[]{:S(2)}) copy-start(bf16[1440,4]{0,1:T(4,128)(2,1)} %copy-done.9) | copy-start | bytes 34564
  235.7 1.6 copy-start.2
  235.7 2.3 copy-start.6
Sparse Core Ops, SparseCore 0:
  199.3 92.8 all-reduce.2
where the time goes:
time: 303 us; the launch traced here: 301 us
  local copies, waits for them, and re-layouts  76.7 us (25%)
  waiting for transfers between devices  64.8 us (21%)
  other arithmetic  34.8 us (11%)
  blocking collectives  33.4 us (11%)
  matrix products  30.5 us (10%)
  starting transfers between devices  22.9 us (8%)
  loops' own time  22.8 us (8%)
  between operations  15 us (5%)
    unnamed x2, waiting for transfers between devices  50.3 us
    unnamed x51, local copies, waits for them, and re-layouts  30.5 us
    another operation x1, loops' own time, legendre_table(): lax.scan(advance, (zeroed, zeroed), jnp.arange(degrees, dtype=jnp.int32))  22.8 us
    dynamic_update_slice x32, other arithmetic, legendre_table(): lax.scan(advance, (zeroed, zeroed), jnp.arange(degrees, dtype=jnp.int32))  21.2 us
    dynamic_slice x32, local copies, waits for them, and re-layouts, legendre_table(): lax.scan(advance, (zeroed, zeroed), jnp.arange(degrees, dtype=jnp.int32))  20.7 us
    all_to_all x1, blocking collectives, to_owners(): lax.all_to_all(values, 'lat', split_axis=0, concat_axis=2, tiled=True)  12.4 us
    all_to_all x2, starting transfers between devices, to_channels(): lax.all_to_all(values, 'lat', split_axis=2, concat_axis=0, tiled=True)  11.6 us
    all_to_all x1, blocking collectives, from_owners(): lax.all_to_all(values, 'lat', split_axis=2, concat_axis=0, tiled=True)  10.5 us
  transfers between devices with their start and end apart: 6, of which 5 were waited for; matrix products, arithmetic and copies ran while one was open for 25% of the time, Pallas kernels for 0%

commit v1 on v0

--- a/solution.py
+++ b/solution.py
@@ -120,7 +120,10 @@
         return lax.all_to_all(values, "lat", split_axis=2, concat_axis=0, tiled=True)
 
     def to_owners(values):
-        return lax.all_to_all(values, "lat", split_axis=0, concat_axis=2, tiled=True)
+        return jnp.concatenate(
+            lax.all_to_all(jnp.stack(jnp.split(values, lax.axis_size("lat"), axis=0)), "lat", 0, 0),
+            axis=2,
+        )
 
     def from_owners(values):
         return lax.all_to_all(values, "lat", split_axis=2, concat_axis=0, tiled=True)

time: 303 us -> 353 us (1.17)
  local copies, waits for them, and re-layouts: 76.7 us -> 146 us
  other arithmetic: 34.8 us -> 14.6 us
    another operation x0 -> x36, local copies, waits for them, and re-layouts: none -> 44.6 us  [to_owners(): jnp.stack(jnp.split(values, lax.axis_size('lat'), axis=0))]
    unnamed x51 -> x81, local copies, waits for them, and re-layouts: 30.5 us -> 60.9 us
    dynamic_update_slice x32, other arithmetic: 21.2 us -> 2.69 us  [legendre_table(): lax.scan(advance, (zeroed, zeroed), jnp.arange(degrees, dtype=jnp.int32))]
    all_to_all x4 -> x0, local copies, waits for them, and re-layouts: 4.87 us -> none  [to_owners(): lax.all_to_all(values, 'lat', split_axis=0, concat_axis=2, tiled=True)]
    reshape x0 -> x4, local copies, waits for them, and re-layouts: none -> 4.87 us  [to_owners(): jnp.concatenate(lax.all_to_all(jnp.stack(jnp.split(values, lax.axis_size(...]
  transfers between devices with their start and end apart: 6 -> 6, of which waited for: 5 -> 5; matrix products, arithmetic and copies ran while one was open for 25% -> 16% of each run, Pallas kernels for 0% -> 0%
where the time goes in v1:
time: 353 us; the launch traced here: 348 us
  local copies, waits for them, and re-layouts  146 us (41%)
  waiting for transfers between devices  65 us (18%)
  blocking collectives  33.8 us (10%)
  matrix products  29.2 us (8%)
  starting transfers between devices  22.9 us (6%)
  loops' own time  22 us (6%)
  between operations  15.1 us (4%)
  other arithmetic  14.6 us (4%)
    unnamed x81, local copies, waits for them, and re-layouts  60.9 us
    unnamed x2, waiting for transfers between devices  50.3 us
    another operation x36, local copies, waits for them, and re-layouts, to_owners(): jnp.stack(jnp.split(values, lax.axis_size('lat'), axis=0))  44.6 us
    another operation x1, loops' own time, legendre_table(): lax.scan(advance, (zeroed, zeroed), jnp.arange(degrees, dtype=jnp.int32))  22 us
    dynamic_slice x32, local copies, waits for them, and re-layouts, legendre_table(): lax.scan(advance, (zeroed, zeroed), jnp.arange(degrees, dtype=jnp.int32))  18.8 us
    all_to_all x1, blocking collectives, to_owners(): lax.all_to_all(jnp.stack(jnp.split(values, lax.axis_size('lat'), axis=0))...  12.6 us
    all_to_all x2, starting transfers between devices, to_channels(): lax.all_to_all(values, 'lat', split_axis=2, concat_axis=0, tiled=True)  11.6 us
    all_to_all x1, blocking collectives, from_owners(): lax.all_to_all(values, 'lat', split_axis=2, concat_axis=0, tiled=True)  10.6 us
  transfers between devices with their start and end apart: 6, of which 5 were waited for; matrix products, arithmetic and copies ran while one was open for 16% of the time, Pallas kernels for 0%

profile of v1, /device:TPU:0, one launch (start us, length us, event | category | flops | bytes accessed | tf_op | source)
XLA Modules:
  0.0 348.1 jit_solution(57159928229270359)
XLA Ops:
  10.6 7.4 %all-to-all-start = ((f32[16,1,384]{2,1,0:T(1,128)}), f32[16,1,384]{2,1,0:T(1,128)}, u32[]{:S(2)}, u32[]{:S(2)}) async-start(f32[16,1,384]{2,1,0:T(1,128)} %reshape.159), calls=%async_computation | async-start | bytes 49152 | tf_op jit(solution)/shard_map/all_to_all | solution.py:120
  18.2 46.4 %while.21 = (s32[]{:T(128)}, f32[4,32]{1,0:T(4,128)S(1)}, f32[4,32]{1,0:T(4,128)S(1)}, f32[32,4,32]{2,1,0:T(4,128)S(1)}, s32[32]{0:T(128)S(1)}, /*index=5*/f32[3...) while((s32[]{:T(128)}, f32[4,32]{1,0:T(4,128)S(1)}, ...), condition=%wide.region_1.2_spmd.clone.clone.clone.clone, body=%wide.region_0.1_spmd.clone.clone.clone.clone.sunk | while | flops 1723 | bytes 15863 | solution.py:63
  66.6 2.0 reduce
  68.6 2.1 reshape.160
  70.7 1.8 copy.46
  76.5 1.5 copy.50
  78.0 1.5 copy.51
  79.5 1.5 copy.52
  81.0 1.5 copy.53
  82.5 1.5 copy.54
  84.0 1.5 copy.55
  85.5 1.5 copy.56
  87.0 1.5 copy.57
  88.5 1.5 copy.58
  90.1 1.5 copy.59
  111.9 1.6 reshape.161
  113.4 12.6 %all_to_all.118 = bf16[16,2,192]{2,1,0:T(2,128)(2,1)} all-to-all(bf16[16,2,192]{2,1,0:T(2,128)(2,1)} %reshape.161), channel_id=1, replica_groups=mesh['grp'=2,'lat'=16] {'lat'}, dimensions={0} | all-to-all | bytes 24576 | tf_op jit(solution)/shard_map/all_to_all | solution.py:124
  126.0 1.5 reshape.162
  127.5 1.5 copy.65
  131.3 1.6 copy.68
  132.9 1.8 reshape.163
  134.6 10.6 %all_to_all.119 = bf16[16,2,192]{2,1,0:T(2,128)(2,1)} all-to-all(bf16[16,2,192]{2,1,0:T(2,128)(2,1)} %reshape.163), channel_id=1, replica_groups=mesh['grp'=2,'lat'=16] {'lat'}, dimensions={0} | all-to-all | bytes 24576 | tf_op jit(solution)/shard_map/all_to_all | solution.py:129
  145.3 1.6 reshape.164
  146.9 1.7 copy.69
  148.5 1.8 fusion.44
  150.4 1.5 copy.72
  151.9 1.6 reshape.165
  153.5 10.6 %all_to_all.120 = bf16[16,2,192]{2,1,0:T(2,128)(2,1)} all-to-all(bf16[16,2,192]{2,1,0:T(2,128)(2,1)} %reshape.165), channel_id=1, replica_groups=mesh['grp'=2,'lat'=16] {'lat'}, dimensions={0} | all-to-all | bytes 24576 | tf_op jit(solution)/shard_map/all_to_all | solution.py:132
  164.1 1.5 reshape.166
  165.6 1.5 copy.73
  167.1 1.6 all_to_all.96
  168.6 1.7 fusion.109
  170.3 4.4 %fusion.33 = bf16[2,1440,384]{2,1,0:T(8,128)(2,1)S(1)} fusion(bf16[2,1440,384]{2,1,0:T(8,128)(2,1)S(1)} %copy-done.5, f32[1440,2,384]{2,0,1:T(8,128)S(1)} %fusion.109, bf16[2,1440,384]{2,1,0:T(8,128)(2,1)S(1)} %copy-done, bf16[384,384]{1,0:T(8,128)(2,1)S(1)} %copy-done.12), kind=kOutput, calls=%fused_computation.45 | convolution fusion | flops 873676800 | bytes 11354112 | tf_op jit(solution)/shard_map/jkc,cd->jkd/dot_general | solution.py:144
  177.1 1.6 copy.74
  178.8 2.2 reshape.167
  180.9 4.1 %all-to-all-start.4 = ((f32[16,1,384]{2,1,0:T(1,128)}), f32[16,1,384]{2,1,0:T(1,128)}, u32[]{:S(2)}, u32[]{:S(2)}) async-start(f32[16,1,384]{2,1,0:T(1,128)} %reshape.167), calls=%async_computation.4 | async-start | bytes 49152 | tf_op jit(solution)/shard_map/all_to_all | solution.py:120
  186.3 5.3 %all-to-all-done.4 = f32[16,1,384]{2,1,0:T(1,128)} async-done(((f32[16,1,384]{2,1,0:T(1,128)}), f32[16,1,384]{2,1,0:T(1,128)}, u32[]{:S(2)}, u32[]{:S(2)}) %all-to-all-start.4) | async-done | bytes 24608 | tf_op jit(solution)/shard_map/all_to_all | solution.py:120
  191.7 2.0 reduce.1
  193.7 2.1 reshape.168
  195.8 1.8 copy.75
  201.6 1.5 copy.79
  203.1 1.5 copy.80
  204.6 1.5 copy.81
  206.1 1.5 copy.82
  207.6 1.5 copy.83
  209.2 1.5 copy.84
  210.7 1.5 copy.85
  212.2 1.5 copy.86
  213.7 1.5 copy.87
  215.2 1.5 copy.88
  237.0 1.6 reshape.169
  238.6 3.7 %all-to-all-start.5 = ((bf16[16,2,192]{2,1,0:T(2,128)(2,1)}), bf16[16,2,192]{2,1,0:T(2,128)(2,1)S(1)}, u32[]{:S(2)}, u32[]{:S(2)}) async-start(bf16[16,2,192]{2,1,0:T(2,128)(2,1)} %reshape.169), calls=%async_computation.5 | async-start | bytes 32768 | tf_op jit(solution)/shard_map/all_to_all | solution.py:124
  242.3 3.8 %convolution_bitcast_fusion = f32[384,384]{0,1:T(8,128)} fusion(bf16[2,1440,384]{2,1,0:T(8,128)(2,1)} %copy-done.1, bf16[2,1440,384]{2,1,0:T(8,128)(2,1)S(1)} %copy-done), kind=kOutput, calls=%fused_computation.56 | convolution fusion | flops 849346560 | bytes 5013504 | tf_op jit(solution)/shard_map/jkc,jkd->cd/dot_general | solution.py:150
  246.2 2.6 all-to-all-done.5
  249.5 1.5 copy.94
  256.4 1.6 copy.95
  258.0 1.8 reshape.171
  259.7 4.1 %all-to-all-start.6 = ((bf16[16,2,192]{2,1,0:T(2,128)(2,1)}), bf16[16,2,192]{2,1,0:T(2,128)(2,1)}, u32[]{:S(2)}, u32[]{:S(2)}) async-start(bf16[16,2,192]{2,1,0:T(2,128)(2,1)} %reshape.171), calls=%async_computation.6 | async-start | bytes 32768 | tf_op jit(solution)/shard_map/all_to_all | solution.py:129
  263.9 2.5 fusion.41
  267.6 2.9 all-to-all-done.6
  272.7 3.5 %all-to-all-start.7 = ((bf16[16,2,192]{2,1,0:T(2,128)(2,1)}), bf16[16,2,192]{2,1,0:T(2,128)(2,1)S(1)}, u32[]{:S(2)}, u32[]{:S(2)}) async-start(bf16[16,2,192]{2,1,0:T(2,128)(2,1)} %reshape.173), calls=%async_computation.7 | async-start | bytes 32768 | tf_op jit(solution)/shard_map/all_to_all | solution.py:132
  278.7 3.9 %all-to-all-done.7 = bf16[16,2,192]{2,1,0:T(2,128)(2,1)S(1)} async-done(((bf16[16,2,192]{2,1,0:T(2,128)(2,1)}), bf16[16,2,192]{2,1,0:T(2,128)(2,1)S(1)}, u32[]{:S(2)}, u32[]{:S(2)}) %all-to-all-start.7) | async-done | bytes 12320 | tf_op jit(solution)/shard_map/all_to_all | solution.py:132
  285.2 3.9 %fusion.38 = bf16[2,1440,384]{2,1,0:T(8,128)(2,1)} fusion(bf16[2,1440,384]{2,1,0:T(8,128)(2,1)S(1)} %copy-done.6, f32[1440,2,384]{2,0,1:T(8,128)S(1)} %fusion.108, bf16[2,1440,384]{2,1,0:T(8,128)(2,1)S(1)} %copy-done.2, bf16[384,384]{1,0:T(8,128)(2,1)} %param.10), kind=kOutput, calls=%fused_computation.50 | convolution fusion | flops 853770240 | bytes 11354112 | tf_op jit(solution)/shard_map/jkd,cd->jkc/dot_general | solution.py:155
  289.1 50.2 %all-reduce.3.cloned.1.call-done = f32[384,384]{0,1:T(8,128)} async-done(((f32[384,384]{0,1:T(8,128)}), f32[384,384]{0,1:T(8,128)}) %all-reduce.3.cloned.1.call-update) | async-done | bytes 589840
  (324 shorter events, 100.3 us)
Async XLA Ops:
  7.2 1.7 copy-start
  7.2 11.1 %copy-start.13 = (f32[4]{0:T(128)S(1)}, f32[4]{0:T(128)}, u32[]{:S(2)}) copy-start(f32[4]{0:T(128)} %constant.106.clone) | copy-start | bytes 52
  7.2 11.0 %copy-start.14 = (s32[32]{0:T(128)S(1)}, s32[32]{0:T(128)}, u32[]{:S(2)}) copy-start(s32[32]{0:T(128)} %param.12) | copy-start | bytes 388
  7.4 0.6 copy-start.9
  7.4 167.3 %copy-start.7 = (bf16[1440,4]{0,1:T(4,128)(2,1)}, bf16[1440,4]{0,1:T(4,128)(2,1)S(1)}, u32[]{:S(2)}) copy-start(bf16[1440,4]{0,1:T(4,128)(2,1)S(1)} %get-tuple-element.365) | copy-start | bytes 34564
  10.6 55.4 %all-to-all-start = ((f32[16,1,384]{2,1,0:T(1,128)}), f32[16,1,384]{2,1,0:T(1,128)}, u32[]{:S(2)}, u32[]{:S(2)}) async-start(f32[16,1,384]{2,1,0:T(1,128)} %reshape.159), calls=%async_computation | async-start | bytes 49152 | tf_op jit(solution)/shard_map/all_to_all | solution.py:120
  66.0 63.9 %copy-start.3 = (bf16[2,2,384,384]{3,2,1,0:T(8,128)(2,1)S(1)}, bf16[2,2,384,384]{3,2,1,0:T(8,128)(2,1)}, u32[]{:S(2)}) copy-start(bf16[2,2,384,384]{3,2,1,0:T(8,128)(2,1)} %param.11) | copy-start | bytes 3538948
  168.6 1.7 copy-start.5
  168.6 1.7 copy-start.12
  170.3 5.8 %copy-start.10 = (bf16[1440,4]{0,1:T(4,128)(2,1)S(1)}, bf16[1440,4]{0,1:T(4,128)(2,1)}, u32[]{:S(2)}) copy-start(bf16[1440,4]{0,1:T(4,128)(2,1)} %copy-done.9) | copy-start | bytes 34564
  174.7 1.4 copy-start.1
  176.1 9.0 %copy-start.15 = (u32[32]{0:T(128)S(1)}, u32[32]{0:T(128)}, u32[]{:S(2)}) copy-start(u32[32]{0:T(128)} %constant.112) | copy-start | bytes 388
  180.9 10.7 %all-to-all-start.4 = ((f32[16,1,384]{2,1,0:T(1,128)}), f32[16,1,384]{2,1,0:T(1,128)}, u32[]{:S(2)}, u32[]{:S(2)}) async-start(f32[16,1,384]{2,1,0:T(1,128)} %reshape.167), calls=%async_computation.4 | async-start | bytes 49152 | tf_op jit(solution)/shard_map/all_to_all | solution.py:120
  238.6 10.1 %all-to-all-start.5 = ((bf16[16,2,192]{2,1,0:T(2,128)(2,1)}), bf16[16,2,192]{2,1,0:T(2,128)(2,1)S(1)}, u32[]{:S(2)}, u32[]{:S(2)}) async-start(bf16[16,2,192]{2,1,0:T(2,128)(2,1)} %reshape.169), calls=%async_computation.5 | async-start | bytes 32768 | tf_op jit(solution)/shard_map/all_to_all | solution.py:124
  242.3 97.1 %all-reduce.3.cloned.1.call-start = ((), (), s32[]{:S(2)}) async-start(), calls=%async_computation.8 | async-start | bytes 1179648
  255.8 10.6 %copy-start.4 = (f32[2,384,384]{2,1,0:T(8,128)S(1)}, f32[2,384,384]{2,1,0:T(8,128)}, u32[]{:S(2)}) copy-start(f32[2,384,384]{2,1,0:T(8,128)} %fusion.92) | copy-start | bytes 3538948
  259.7 10.7 %all-to-all-start.6 = ((bf16[16,2,192]{2,1,0:T(2,128)(2,1)}), bf16[16,2,192]{2,1,0:T(2,128)(2,1)}, u32[]{:S(2)}, u32[]{:S(2)}) async-start(bf16[16,2,192]{2,1,0:T(2,128)(2,1)} %reshape.171), calls=%async_computation.6 | async-start | bytes 32768 | tf_op jit(solution)/shard_map/all_to_all | solution.py:129
  272.7 10.0 %all-to-all-start.7 = ((bf16[16,2,192]{2,1,0:T(2,128)(2,1)}), bf16[16,2,192]{2,1,0:T(2,128)(2,1)S(1)}, u32[]{:S(2)}, u32[]{:S(2)}) async-start(bf16[16,2,192]{2,1,0:T(2,128)(2,1)} %reshape.173), calls=%async_computation.7 | async-start | bytes 32768 | tf_op jit(solution)/shard_map/all_to_all | solution.py:132
  276.2 6.7 %copy-start.8 = (bf16[1440,4]{0,1:T(4,128)(2,1)S(1)}, bf16[1440,4]{0,1:T(4,128)(2,1)}, u32[]{:S(2)}) copy-start(bf16[1440,4]{0,1:T(4,128)(2,1)} %copy-done.7) | copy-start | bytes 34564
  276.2 6.7 %copy-start.11 = (bf16[1440,4]{0,1:T(4,128)(2,1)S(1)}, bf16[1440,4]{0,1:T(4,128)(2,1)}, u32[]{:S(2)}) copy-start(bf16[1440,4]{0,1:T(4,128)(2,1)} %copy-done.9) | copy-start | bytes 34564
  282.9 1.6 copy-start.2
  282.9 2.3 copy-start.6
Sparse Core Ops, SparseCore 0:
  246.5 92.8 all-reduce.2
